TPU v7x, 32 devices: a whole 2x2x4 slice. The times are simulated.
32 devices in a mesh: dp: 4 (over y, x), seq: 8 (over z, core).
Axes of the slice: x: 2, y: 2, z: 4, core: 2. Of those that a mesh axis runs over, the one named last changes fastest.
Arguments:
- asking_vectors_matrix: bfloat16 [4, 1024, 2048], P('dp', 'seq'), may hold values from -6 to 6
- matched_keys_matrix: bfloat16 [4, 1024, 2048], P('dp', 'seq'), may hold values from -6 to 6
- carried_vectors_matrix: bfloat16 [4, 1024, 2048], P('dp', 'seq'), may hold values from -6 to 6
- upstream_cotangent: bfloat16 [4, 1024, 2048], P('dp', 'seq'), may hold values from -6 to 6
- w_out: bfloat16 [2048, 2048], P('seq'), may hold values from -0.125 to 0.125
- panel_entry_offsets: int32 [4, 9], P('dp'), may hold values from 0 to 32, as said below
- rightward_panel_per_entry: int32 [4, 32], P('dp'), may hold values from 0 to 7, as said below
Outputs:
- layer_out: bfloat16 [4, 1024, 2048], P('dp', 'seq')
- q_grad: bfloat16 [4, 1024, 2048], P('dp', 'seq')
- k_grad: bfloat16 [4, 1024, 2048], P('dp', 'seq')
- v_grad: bfloat16 [4, 1024, 2048], P('dp', 'seq')
- w_out_grad: float32 [2048, 2048], P('seq')
Inputs may be any that keep to these rules, and one draw needn't show every extreme that they name: panel_entry_offsets[b, 0] is 0 and panel_entry_offsets never falls along a row; tile row r owns slots panel_entry_offsets[b, r] to panel_entry_offsets[b, r + 1] - 1, 1 to 8 of them, and its own tile r is among its blocks; in every subgraph one tile row holds all 8 tiles; panel_entry_offsets[b, 8], the used slots, lies between 16 and 32 and equals 32 for at least one subgraph. `rightward_panel_per_entry`: the slots of a tile row hold distinct column tiles in rising order; slots from panel_entry_offsets[b, 8] on hold arbitrary tile numbers that take no part.
All inputs are finite; a program needn't handle non-finite values.
Results may differ from a plain program's by a relative error of at most 0.034.
Values may be sent and summed in bfloat16 or wider, within the bound.
No kernel may reach another device: no remote copies, remote signals or barrier semaphores. Data moves between devices by JAX's collectives and lax.ppermute only.
A program may use at most 128 MiB of HBM per device.

v0:
```python
import math
import jax
import jax.numpy as jnp
from jax import lax
from jax.sharding import PartitionSpec as P

H = 16
HD = 128


def tile_mask(starts, columns, nodes):
    tile_count = starts.shape[0] - 1
    slot_count = columns.shape[0]
    tile_size = nodes // tile_count
    slot_index = jnp.arange(slot_count, dtype=jnp.int32)
    entry_row = jnp.sum((starts[1:][None, :] <= slot_index[:, None]).astype(jnp.int32), axis=1)
    tile_ids = jnp.arange(tile_count, dtype=jnp.int32)
    row_hot = (entry_row[:, None] == tile_ids[None, :]).astype(jnp.int32)
    col_hot = (columns[:, None] == tile_ids[None, :]).astype(jnp.int32)
    pairs = jnp.einsum("er,ec->rc", row_hot, col_hot) > 0
    full = jnp.broadcast_to(pairs[:, None, :, None], (tile_count, tile_size, tile_count, tile_size))
    return jnp.where(full.reshape(nodes, nodes), 0.0, -jnp.inf)


def attend(q, k, v, allowed):
    factor = 1.0 / math.sqrt(q.shape[-1])
    scores = jnp.dot(q, k.T, preferred_element_type=jnp.float32) * factor
    masked = scores + allowed
    row_max = jnp.max(masked, axis=1, keepdims=True)
    expd = jnp.exp(masked - row_max)
    row_total = jnp.sum(expd, axis=1, keepdims=True)
    weighted = jnp.dot(expd.astype(jnp.bfloat16), v, preferred_element_type=jnp.float32)
    attended = (weighted / row_total).astype(jnp.bfloat16)
    return (attended, expd, row_total)


def attend_back(q, k, v, g, attended, expd, row_total):
    factor = 1.0 / math.sqrt(q.shape[-1])
    prob = expd * (1.0 / row_total)
    prob_low = prob.astype(jnp.bfloat16)
    v_grad = jnp.dot(prob_low.T, g, preferred_element_type=jnp.float32)
    prob_grad = jnp.dot(g, v.T, preferred_element_type=jnp.float32)
    delta = jnp.sum(attended.astype(jnp.float32) * g.astype(jnp.float32), axis=1, keepdims=True)
    score_grad = (prob * (prob_grad - delta) * factor).astype(jnp.bfloat16)
    q_grad = jnp.dot(score_grad, k, preferred_element_type=jnp.float32)
    k_grad = jnp.dot(score_grad.T, q, preferred_element_type=jnp.float32)
    return (q_grad.astype(jnp.bfloat16), k_grad.astype(jnp.bfloat16), v_grad.astype(jnp.bfloat16))


def chip_layer_out(att_flat, w_out):
    n = lax.axis_size("seq")
    rows = att_flat.shape[0] // n
    chips = n // 2
    s = lax.axis_index("seq")
    core = s % 2
    z = s // 2
    sibling = [(i, i ^ 1) for i in range(n)]
    att_sib = lax.ppermute(att_flat, "seq", sibling)
    w_sib = lax.ppermute(w_out, "seq", sibling)

    def parity_rows(values):
        quads = values.reshape(chips, 2, rows, values.shape[1])
        return jnp.where(core == 0, quads[:, 0], quads[:, 1])

    att_chip = jnp.concatenate([parity_rows(att_flat), parity_rows(att_sib)], axis=2)
    w_chip = jnp.concatenate([w_out, w_sib], axis=0)
    chip_partial = lax.dot_general(
        att_chip, w_chip, (((2,), (0,)), ((), ())), preferred_element_type=jnp.float32
    )
    total = lax.dynamic_index_in_dim(chip_partial, z, 0, keepdims=False)
    sent = chip_partial.astype(jnp.bfloat16)
    for k in range(1, chips):
        pairs = [(i, (i // 2 + k) % chips * 2 + i % 2) for i in range(n)]
        piece = lax.dynamic_index_in_dim(sent, (z + k) % chips, 0, keepdims=False)
        total = total + lax.ppermute(piece, "seq", pairs).astype(jnp.float32)
    return total


def shards(
    asking_vectors_matrix,
    matched_keys_matrix,
    carried_vectors_matrix,
    upstream_cotangent,
    w_out,
    panel_entry_offsets,
    rightward_panel_per_entry,
):
    nodes_here = asking_vectors_matrix.shape[1]
    width = asking_vectors_matrix.shape[2]
    n_seq = lax.axis_size("seq")
    nodes = nodes_here * n_seq
    grad_here = upstream_cotangent[0]
    grad_full = lax.all_gather(grad_here, "seq", axis=0, tiled=True)
    groups = n_seq
    group_width = width // groups
    local_heads = group_width // HD

    def to_groups(values):
        return values.reshape(nodes_here, groups, group_width).transpose(1, 0, 2)

    stacked = jnp.stack(
        [
            to_groups(asking_vectors_matrix[0]),
            to_groups(matched_keys_matrix[0]),
            to_groups(carried_vectors_matrix[0]),
        ]
    )
    heads = lax.all_to_all(stacked, "seq", split_axis=1, concat_axis=1, tiled=True)
    heads = heads.reshape(3, nodes, group_width)
    allowed = tile_mask(panel_entry_offsets[0], rightward_panel_per_entry[0], nodes)

    def head_cols(values, h):
        return values[:, h * HD : (h + 1) * HD]

    fwd = [
        attend(head_cols(heads[0], h), head_cols(heads[1], h), head_cols(heads[2], h), allowed)
        for h in range(local_heads)
    ]
    att_flat = jnp.concatenate([f[0] for f in fwd], axis=1)
    layer_out = chip_layer_out(att_flat, w_out).astype(jnp.bfloat16)[None]
    g_flat = lax.dot_general(
        grad_full, w_out, (((1,), (1,)), ((), ())), preferred_element_type=jnp.float32
    ).astype(jnp.bfloat16)
    att_blocks = att_flat.reshape(n_seq, nodes_here, local_heads * HD)
    grad_blocks = grad_full.reshape(n_seq, nodes_here, width)
    terms = jnp.einsum(
        "bnf,bnk->bfk", att_blocks, grad_blocks, preferred_element_type=jnp.float32
    ).astype(jnp.bfloat16)
    w_rows = jnp.sum(terms.astype(jnp.float32), axis=0)
    w_rows = lax.psum(w_rows.astype(jnp.bfloat16), "dp").astype(jnp.float32)
    batch = asking_vectors_matrix.shape[0] * lax.axis_size("dp")
    w_out_grad = w_rows / batch
    bwd = [
        attend_back(
            head_cols(heads[0], h),
            head_cols(heads[1], h),
            head_cols(heads[2], h),
            head_cols(g_flat, h),
            fwd[h][0],
            fwd[h][1],
            fwd[h][2],
        )
        for h in range(local_heads)
    ]
    grads = jnp.stack(
        [
            jnp.concatenate([b[i] for b in bwd], axis=1).reshape(groups, nodes_here, group_width)
            for i in range(3)
        ]
    )
    back = lax.all_to_all(grads, "seq", split_axis=1, concat_axis=1, tiled=True)
    back = back.transpose(0, 2, 1, 3).reshape(3, 1, nodes_here, width)
    return (layer_out, back[0], back[1], back[2], w_out_grad)


def solution(mesh):
    return jax.shard_map(
        shards,
        mesh=mesh,
        in_specs=(
            P("dp", "seq", None),
            P("dp", "seq", None),
            P("dp", "seq", None),
            P("dp", "seq", None),
            P("seq", None),
            P("dp", None),
            P("dp", None),
        ),
        out_specs=(
            P("dp", "seq", None),
            P("dp", "seq", None),
            P("dp", "seq", None),
            P("dp", "seq", None),
            P("seq", None),
        ),
        check_vma=False,
    )
```

profile of v0, /device:TPU:10, one launch (start us, length us, event | category | flops | bytes accessed | tf_op | source)
XLA Modules:
  0.0 211.3 jit_solution(6985377320653367382)
XLA Ops:
  7.9 1.3 copy.72
  9.2 1.3 copy.73
  10.5 1.3 copy.74
  12.1 1.2 copy.75
  13.3 5.3 %all-to-all-start = ((bf16[3,8,128,256]{2,3,0,1:T(8,128)(2,1)}), bf16[3,8,128,256]{2,3,0,1:T(8,128)(2,1)S(1)}, u32[]{:S(2)}, u32[]{:S(2)}) async-start(bf16[3,8,128,256]{2,3,0,1:T(8,128)(2,1)} %copy.75), calls=%async_computation | async-start | bytes 3145728 | tf_op jit(solution)/shard_map/all_to_all | solution.py:108
  19.3 67.4 %all-to-all-done = bf16[3,8,128,256]{2,3,0,1:T(8,128)(2,1)S(1)} async-done(((bf16[3,8,128,256]{2,3,0,1:T(8,128)(2,1)}), bf16[3,8,128,256]{2,3,0,1:T(8,128)(2,1)S(1)}, u32[]{:S(2)}, u32[]{:S(2)}) %all-to-all-start) | async-done | bytes 1572896 | tf_op jit(solution)/shard_map/all_to_all | solution.py:108
  87.9 1.2 fusion.73
  91.7 1.3 copy-done.2
  93.9 3.9 %fusion.21 = bf16[1024,256]{0,1:T(8,128)(2,1)S(1)} fusion(bf16[256,2048]{1,0:T(8,128)(2,1)} %param.11, bf16[1,1024,2048]{2,1,0:T(8,128)(2,1)} %all-gather.3.cloned.1.call-done), kind=kOutput, calls=%fused_computation.32 | convolution fusion | flops 1074003968 | bytes 5767168 | tf_op jit(solution)/shard_map/dot_general | solution.py:121
  108.8 1.4 pad_maximum_fusion.1
  110.1 6.9 %all-to-all-start.1 = ((bf16[3,8,128,256]{2,3,0,1:T(8,128)(2,1)}), bf16[3,8,128,256]{2,3,0,1:T(8,128)(2,1)S(1)}, u32[]{:S(2)}, u32[]{:S(2)}) async-start(bf16[3,8,128,256]{2,3,0,1:T(8,128)(2,1)} %pad_maximum_fusion.1), calls=%async_computation.1 | async-start | bytes 3145728 | tf_op jit(solution)/shard_map/all_to_all | solution.py:151
  117.0 1.5 fusion.70
  118.5 1.2 copy.98
  120.9 5.9 %convert_reduce_fusion = bf16[256,2048]{1,0:T(8,128)(2,1)} fusion(bf16[8,128,2048]{2,1,0:T(8,128)(2,1)} %bitcast.122, bf16[32,8,8,128]{3,2,1,0:T(8,128)(2,1)} %get-tuple-element.26), kind=kOutput, calls=%fused_computation | convolution fusion | flops 1081606144 | bytes 5767168 | tf_op jit(solution)/shard_map/bnf,bnk->bfk/dot_general | solution.py:126
  126.8 1.4 reshape.64
  130.0 4.7 %fusion.74 = (bf16[4,128,2048]{2,1,0:T(8,128)(2,1)S(1)}, f32[4,128,2048]{2,1,0:T(8,128)}) fusion(bf16[256,2048]{1,0:T(8,128)(2,1)} %collective-permute-done.1, bf16[256,2048]{1,0:T(8,128)(2,1)} %param.11, bf16[4,128,256]{2,1,0:T(8,128)(2,1)S(1)} %get-tuple-element.39, bf16[4,128,256]{2,1,0:T(8,128)(2,1)S(1)} %get-tuple-element.40), kind=kOutput, calls=%fused_computation.99 | convolution fusion | flops 1080033280 | bytes 8912896 | tf_op jit(solution)/shard_map/dot_general | solution.py:67
  134.9 1.5 collective-permute-start.2
  137.5 1.9 collective-permute-start.4
  139.4 41.1 %all-reduce.2.cloned.1.call-done = bf16[256,2048]{1,0:T(8,128)(2,1)} async-done(((bf16[256,2048]{1,0:T(8,128)(2,1)}), bf16[256,2048]{1,0:T(8,128)(2,1)}) %all-reduce.2.cloned.1.call-update) | async-done | bytes 1048592 | tf_op jit(solution)/shard_map/psum | solution.py:130
  180.4 2.8 %convert_multiply_fusion = f32[256,2048]{1,0:T(8,128)} fusion(bf16[256,2048]{1,0:T(8,128)(2,1)} %all-reduce.2.cloned.1.call-done), kind=kLoop, calls=%fused_computation.23 | loop fusion | flops 1048576 | bytes 3145728 | tf_op jit(solution)/shard_map/div | solution.py:132
  183.2 1.9 collective-permute-done.2
  185.1 11.2 %collective-permute-done.3 = bf16[128,2048]{1,0:T(8,128)(2,1)} collective-permute-done((bf16[128,2048]{1,0:T(8,128)(2,1)S(1)}, bf16[128,2048]{1,0:T(8,128)(2,1)}, u32[]{:S(2)}, u32[]{:S(2)}) %collective-permute-start.3) | collective-permute-done | bytes 524320 | tf_op jit(solution)/shard_map/ppermute | solution.py:75
  196.3 2.2 %collective-permute-done.4 = bf16[128,2048]{1,0:T(8,128)(2,1)} collective-permute-done((bf16[128,2048]{1,0:T(8,128)(2,1)S(1)}, bf16[128,2048]{1,0:T(8,128)(2,1)}, u32[]{:S(2)}, u32[]{:S(2)}) %collective-permute-start.4) | collective-permute-done | bytes 524320 | tf_op jit(solution)/shard_map/ppermute | solution.py:75
  198.5 2.8 %fusion.42 = bf16[1,128,2048]{2,1,0:T(8,128)(2,1)} fusion(bf16[128,2048]{1,0:T(8,128)(2,1)} %collective-permute-done.4, bf16[128,2048]{1,0:T(8,128)(2,1)} %collective-permute-done.3, bf16[128,2048]{1,0:T(8,128)(2,1)} %collective-permute-done.2, f32[4,128,2048]{2,1,0:T(8,128)} %get-tuple-element.37, s32[]{:T(128)S(6)} %select_n.72), kind=kLoop, calls=%fused_computation.49 | loop fusion | flops 1835008 | bytes 3145732 | tf_op jit(solution)/shard_map/broadcast_in_dim | solution.py:120
  (68 shorter events, 24.2 us)
Async XLA Ops:
  7.2 86.7 %all-gather.3.cloned.1.call-start = ((), (), s32[]{:S(2)}) async-start(), calls=%async_computation.3 | async-start | bytes 4718592 | tf_op jit(solution)/shard_map/all_gather | solution.py:93
  11.9 6.9 %copy-start.4 = (s32[1,9]{1,0:T(1,128)S(1)}, s32[1,9]{1,0:T(1,128)}, u32[]{:S(2)}) copy-start(s32[1,9]{1,0:T(1,128)} %param.12) | copy-start | bytes 112
  11.9 7.1 %copy-start.5 = (s32[1,32]{1,0:T(1,128)S(1)}, s32[1,32]{1,0:T(1,128)}, u32[]{:S(2)}) copy-start(s32[1,32]{1,0:T(1,128)} %param.13) | copy-start | bytes 388
  13.3 73.4 %all-to-all-start = ((bf16[3,8,128,256]{2,3,0,1:T(8,128)(2,1)}), bf16[3,8,128,256]{2,3,0,1:T(8,128)(2,1)S(1)}, u32[]{:S(2)}, u32[]{:S(2)}) async-start(bf16[3,8,128,256]{2,3,0,1:T(8,128)(2,1)} %copy.75), calls=%async_computation | async-start | bytes 3145728 | tf_op jit(solution)/shard_map/all_to_all | solution.py:108
  18.6 111.3 %collective-permute-start.1 = (bf16[256,2048]{1,0:T(8,128)(2,1)}, bf16[256,2048]{1,0:T(8,128)(2,1)}, u32[]{:S(2)}, u32[]{:S(2)}) collective-permute-start(bf16[256,2048]{1,0:T(8,128)(2,1)} %param.11), channel_id=1, source_target_pairs={{0,1},{1,0},{2,3},{3,2},{4,5},{5,4},{6,7},{7,6},{8,9},{9,8},{10,11... | collective-permute-start | bytes 3145736 | tf_op jit(solution)/shard_map/ppermute | solution.py:59
  89.1 2.0 copy-start
  91.1 2.0 copy-start.2
  93.9 3.9 %copy-start.1 = (f32[1024,1024]{0,1:T(8,128)S(1)}, f32[1024,1024]{0,1:T(8,128)}, u32[]{:S(2)}) copy-start(f32[1024,1024]{0,1:T(8,128)} %copy-done) | copy-start | bytes 12582916
  99.9 2.2 %copy-start.3 = (f32[1024,1024]{0,1:T(8,128)S(1)}, f32[1024,1024]{0,1:T(8,128)}, u32[]{:S(2)}) copy-start(f32[1024,1024]{0,1:T(8,128)} %copy-done.2) | copy-start | bytes 12582916
  107.6 19.1 %collective-permute-start = (bf16[1024,256]{0,1:T(8,128)(2,1)S(1)}, bf16[1024,256]{0,1:T(8,128)(2,1)}, u32[]{:S(2)}, u32[]{:S(2)}) collective-permute-start(bf16[1024,256]{0,1:T(8,128)(2,1)S(1)} %get-tuple-element.27), channel_id=1, source_target_pairs={{0,1},{1,0},{2,3},{3,2},{4,5},{5,4},{6,7},{7,6},{8,9},{9,8},{10,11... | collective-permute-start | bytes 1572872 | tf_op jit(solution)/shard_map/ppermute | solution.py:58
  110.1 91.2 %all-to-all-start.1 = ((bf16[3,8,128,256]{2,3,0,1:T(8,128)(2,1)}), bf16[3,8,128,256]{2,3,0,1:T(8,128)(2,1)S(1)}, u32[]{:S(2)}, u32[]{:S(2)}) async-start(bf16[3,8,128,256]{2,3,0,1:T(8,128)(2,1)} %pad_maximum_fusion.1), calls=%async_computation.1 | async-start | bytes 3145728 | tf_op jit(solution)/shard_map/all_to_all | solution.py:151
  117.0 63.4 %all-reduce.2.cloned.1.call-start = ((), (), s32[]{:S(2)}) async-start(), calls=%async_computation.2 | async-start | bytes 2097152 | tf_op jit(solution)/shard_map/psum | solution.py:130
  134.9 50.2 %collective-permute-start.2 = (bf16[128,2048]{1,0:T(8,128)(2,1)S(1)}, bf16[128,2048]{1,0:T(8,128)(2,1)}, u32[]{:S(2)}, u32[]{:S(2)}) collective-permute-start(bf16[128,2048]{1,0:T(8,128)(2,1)S(1)} %get-tuple-element.17), channel_id=1, source_target_pairs={{0,2},{1,3},{2,4},{3,5},{4,6},{5,7},{6,0},{7,1},{8,10},{9,11},{10,... | collective-permute-start | bytes 1572872 | tf_op jit(solution)/shard_map/ppermute | solution.py:75
  136.4 59.8 %collective-permute-start.3 = (bf16[128,2048]{1,0:T(8,128)(2,1)S(1)}, bf16[128,2048]{1,0:T(8,128)(2,1)}, u32[]{:S(2)}, u32[]{:S(2)}) collective-permute-start(bf16[128,2048]{1,0:T(8,128)(2,1)S(1)} %get-tuple-element.19), channel_id=1, source_target_pairs={{0,4},{1,5},{2,6},{3,7},{4,0},{5,1},{6,2},{7,3},{8,12},{9,13},{10,... | collective-permute-start | bytes 1572872 | tf_op jit(solution)/shard_map/ppermute | solution.py:75
  137.5 61.0 %collective-permute-start.4 = (bf16[128,2048]{1,0:T(8,128)(2,1)S(1)}, bf16[128,2048]{1,0:T(8,128)(2,1)}, u32[]{:S(2)}, u32[]{:S(2)}) collective-permute-start(bf16[128,2048]{1,0:T(8,128)(2,1)S(1)} %get-tuple-element.18), channel_id=1, source_target_pairs={{0,6},{1,7},{2,0},{3,1},{4,2},{5,3},{6,4},{7,5},{8,14},{9,15},{10,... | collective-permute-start | bytes 1572872 | tf_op jit(solution)/shard_map/ppermute | solution.py:75
Sparse Core Ops, SparseCore 0:
  9.6 77.0 all-gather.2
  126.9 53.4 all-reduce.1
where the time goes:
time: 212 us; the launch traced here: 211 us
  waiting for transfers between devices  124 us (58%)
  matrix products  25.9 us (12%)
  local copies, waits for them, and re-layouts  19.9 us (9%)
  starting transfers between devices  17 us (8%)
  between operations  14.4 us (7%)
  other arithmetic  9.61 us (5%)
    all_to_all x1, waiting for transfers between devices, shards(): lax.all_to_all(stacked, 'seq', split_axis=1, concat_axis=1, tiled=True)  67.4 us
    psum x1, waiting for transfers between devices, shards(): w_rows = lax.psum(w_rows.astype(jnp.bfloat16), 'dp').astype(jnp.float32)  41.1 us
    ppermute x3, waiting for transfers between devices, chip_layer_out(): total = total + lax.ppermute(piece, 'seq', pairs).astype(jnp.float32)  15.3 us
    unnamed x28, local copies, waits for them, and re-layouts  13.5 us
    all_to_all x1, starting transfers between devices, shards(): back = lax.all_to_all(grads, 'seq', split_axis=1, concat_axis=1, tiled=True)  6.9 us
    dot_general x1, matrix products, shards(): jnp.einsum('bnf,bnk->bfk', att_blocks, grad_blocks, preferred_element_typ...  5.87 us
    all_to_all x1, starting transfers between devices, shards(): lax.all_to_all(stacked, 'seq', split_axis=1, concat_axis=1, tiled=True)  5.32 us
    dot_general x1, matrix products, chip_layer_out(): lax.dot_general(att_chip, w_chip, (((2,), (0,)), ((), ())), preferred_ele...  4.73 us
  transfers between devices with their start and end apart: 9, of which 5 were waited for; matrix products, arithmetic and copies ran while one was open for 24% of the time, Pallas kernels for 0%

commit v1 on v0

--- a/solution.py
+++ b/solution.py
@@ -148,7 +148,10 @@
             for i in range(3)
         ]
     )
-    back = lax.all_to_all(grads, "seq", split_axis=1, concat_axis=1, tiled=True)
+    size = lax.axis_size("seq")
+    blocks = jnp.stack(jnp.split(grads, size, axis=1), axis=0)
+    blocks = lax.all_to_all(blocks, "seq", split_axis=0, concat_axis=0)
+    back = jnp.concatenate(blocks, axis=1)
     back = back.transpose(0, 2, 1, 3).reshape(3, 1, nodes_here, width)
     return (layer_out, back[0], back[1], back[2], w_out_grad)
 

time: 212 us -> 220 us (1.038)
  local copies, waits for them, and re-layouts: 19.9 us -> 26.4 us
    unnamed x28 -> x34, local copies, waits for them, and re-layouts: 13.5 us -> 18.1 us
  transfers between devices with their start and end apart: 9 -> 9, of which waited for: 5 -> 5; matrix products, arithmetic and copies ran while one was open for 24% -> 26% of each run, Pallas kernels for 0% -> 0%
where the time goes in v1:
time: 220 us; the launch traced here: 219 us
  waiting for transfers between devices  124 us (56%)
  matrix products  27.4 us (12%)
  local copies, waits for them, and re-layouts  26.4 us (12%)
  starting transfers between devices  17 us (8%)
  between operations  14.4 us (7%)
  other arithmetic  9.38 us (4%)
    all_to_all x1, waiting for transfers between devices, shards(): lax.all_to_all(stacked, 'seq', split_axis=1, concat_axis=1, tiled=True)  67.4 us
    psum x1, waiting for transfers between devices, shards(): w_rows = lax.psum(w_rows.astype(jnp.bfloat16), 'dp').astype(jnp.float32)  41 us
    unnamed x34, local copies, waits for them, and re-layouts  18.1 us
    ppermute x3, waiting for transfers between devices, chip_layer_out(): total = total + lax.ppermute(piece, 'seq', pairs).astype(jnp.float32)  15.3 us
    all_to_all x1, starting transfers between devices, shards(): blocks = lax.all_to_all(blocks, 'seq', split_axis=0, concat_axis=0)  6.91 us
    dot_general x1, matrix products, shards(): jnp.einsum('bnf,bnk->bfk', att_blocks, grad_blocks, preferred_element_typ...  5.87 us
    all_to_all x1, starting transfers between devices, shards(): lax.all_to_all(stacked, 'seq', split_axis=1, concat_axis=1, tiled=True)  5.32 us
    dot_general x1, matrix products, chip_layer_out(): lax.dot_general(att_chip, w_chip, (((2,), (0,)), ((), ())), preferred_ele...  4.75 us
  transfers between devices with their start and end apart: 9, of which 5 were waited for; matrix products, arithmetic and copies ran while one was open for 26% of the time, Pallas kernels for 0%

profile of v1, /device:TPU:10, one launch (start us, length us, event | category | flops | bytes accessed | tf_op | source)
XLA Modules:
  0.0 219.0 jit_solution(15903925227728876794)
XLA Ops:
  7.9 1.3 copy.88
  9.2 1.3 copy.89
  10.5 1.3 copy.90
  12.1 1.2 copy.91
  13.3 5.3 %all-to-all-start = ((bf16[3,8,128,256]{2,3,0,1:T(8,128)(2,1)}), bf16[3,8,128,256]{2,3,0,1:T(8,128)(2,1)S(1)}, u32[]{:S(2)}, u32[]{:S(2)}) async-start(bf16[3,8,128,256]{2,3,0,1:T(8,128)(2,1)} %copy.91), calls=%async_computation | async-start | bytes 3145728 | tf_op jit(solution)/shard_map/all_to_all | solution.py:108
  19.3 67.4 %all-to-all-done = bf16[3,8,128,256]{2,3,0,1:T(8,128)(2,1)S(1)} async-done(((bf16[3,8,128,256]{2,3,0,1:T(8,128)(2,1)}), bf16[3,8,128,256]{2,3,0,1:T(8,128)(2,1)S(1)}, u32[]{:S(2)}, u32[]{:S(2)}) %all-to-all-start) | async-done | bytes 1572896 | tf_op jit(solution)/shard_map/all_to_all | solution.py:108
  87.9 1.2 fusion.81
  91.7 1.3 copy-done.2
  93.9 3.9 %fusion.21 = bf16[1024,256]{0,1:T(8,128)(2,1)S(1)} fusion(bf16[256,2048]{1,0:T(8,128)(2,1)} %param.11, bf16[1,1024,2048]{2,1,0:T(8,128)(2,1)} %all-gather.3.cloned.1.call-done), kind=kOutput, calls=%fused_computation.32 | convolution fusion | flops 1074003968 | bytes 5767168 | tf_op jit(solution)/shard_map/dot_general | solution.py:121
  106.5 1.6 fusion.30
  117.0 6.9 %all-to-all-start.1 = ((bf16[8,3,1,128,256]{4,3,1,2,0:T(8,128)(2,1)}), bf16[8,3,1,128,256]{4,3,1,2,0:T(8,128)(2,1)S(1)}, u32[]{:S(2)}, u32[]{:S(2)}) async-start(bf16[8,3,1,128,256]{4,3,1,2,0:T(8,128)(2,1)} %fusion.64), calls=%async_computation.1 | async-start | bytes 3145728 | tf_op jit(solution)/shard_map/all_to_all | solution.py:153
  123.9 1.5 fusion.78
  125.4 1.2 copy.120
  127.8 5.9 %convert_reduce_fusion = bf16[256,2048]{1,0:T(8,128)(2,1)} fusion(bf16[8,128,2048]{2,1,0:T(8,128)(2,1)} %bitcast.143, bf16[32,8,8,128]{3,2,1,0:T(8,128)(2,1)} %get-tuple-element.31), kind=kOutput, calls=%fused_computation | convolution fusion | flops 1081606144 | bytes 5767168 | tf_op jit(solution)/shard_map/bnf,bnk->bfk/dot_general | solution.py:126
  133.7 1.4 reshape.70
  136.9 4.7 %fusion.82 = (bf16[4,128,2048]{2,1,0:T(8,128)(2,1)S(1)}, f32[4,128,2048]{2,1,0:T(8,128)}) fusion(bf16[256,2048]{1,0:T(8,128)(2,1)} %collective-permute-done.1, bf16[256,2048]{1,0:T(8,128)(2,1)} %param.11, bf16[4,128,256]{2,1,0:T(8,128)(2,1)S(1)} %get-tuple-element.44, bf16[4,128,256]{2,1,0:T(8,128)(2,1)S(1)} %get-tuple-element.45), kind=kOutput, calls=%fused_computation.115 | convolution fusion | flops 1080033280 | bytes 8912896 | tf_op jit(solution)/shard_map/dot_general | solution.py:67
  141.8 1.5 collective-permute-start.2
  144.4 1.9 collective-permute-start.4
  146.3 41.0 %all-reduce.2.cloned.1.call-done = bf16[256,2048]{1,0:T(8,128)(2,1)} async-done(((bf16[256,2048]{1,0:T(8,128)(2,1)}), bf16[256,2048]{1,0:T(8,128)(2,1)}) %all-reduce.2.cloned.1.call-update) | async-done | bytes 1048592 | tf_op jit(solution)/shard_map/psum | solution.py:130
  187.3 2.8 %convert_multiply_fusion = f32[256,2048]{1,0:T(8,128)} fusion(bf16[256,2048]{1,0:T(8,128)(2,1)} %all-reduce.2.cloned.1.call-done), kind=kLoop, calls=%fused_computation.23 | loop fusion | flops 1048576 | bytes 3145728 | tf_op jit(solution)/shard_map/div | solution.py:132
  190.1 1.9 collective-permute-done.2
  192.0 11.2 %collective-permute-done.3 = bf16[128,2048]{1,0:T(8,128)(2,1)} collective-permute-done((bf16[128,2048]{1,0:T(8,128)(2,1)S(1)}, bf16[128,2048]{1,0:T(8,128)(2,1)}, u32[]{:S(2)}, u32[]{:S(2)}) %collective-permute-start.3) | collective-permute-done | bytes 524320 | tf_op jit(solution)/shard_map/ppermute | solution.py:75
  203.2 2.2 %collective-permute-done.4 = bf16[128,2048]{1,0:T(8,128)(2,1)} collective-permute-done((bf16[128,2048]{1,0:T(8,128)(2,1)S(1)}, bf16[128,2048]{1,0:T(8,128)(2,1)}, u32[]{:S(2)}, u32[]{:S(2)}) %collective-permute-start.4) | collective-permute-done | bytes 524320 | tf_op jit(solution)/shard_map/ppermute | solution.py:75
  205.4 2.8 %fusion.42 = bf16[1,128,2048]{2,1,0:T(8,128)(2,1)} fusion(bf16[128,2048]{1,0:T(8,128)(2,1)} %collective-permute-done.4, bf16[128,2048]{1,0:T(8,128)(2,1)} %collective-permute-done.3, bf16[128,2048]{1,0:T(8,128)(2,1)} %collective-permute-done.2, f32[4,128,2048]{2,1,0:T(8,128)} %get-tuple-element.42, s32[]{:T(128)S(6)} %select_n.72), kind=kLoop, calls=%fused_computation.49 | loop fusion | flops 1835008 | bytes 3145732 | tf_op jit(solution)/shard_map/broadcast_in_dim | solution.py:120
  (78 shorter events, 31.6 us)
Async XLA Ops:
  7.2 86.7 %all-gather.3.cloned.1.call-start = ((), (), s32[]{:S(2)}) async-start(), calls=%async_computation.3 | async-start | bytes 4718592 | tf_op jit(solution)/shard_map/all_gather | solution.py:93
  11.9 6.9 %copy-start.5 = (s32[1,9]{1,0:T(1,128)S(1)}, s32[1,9]{1,0:T(1,128)}, u32[]{:S(2)}) copy-start(s32[1,9]{1,0:T(1,128)} %param.12) | copy-start | bytes 112
  11.9 7.1 %copy-start.6 = (s32[1,32]{1,0:T(1,128)S(1)}, s32[1,32]{1,0:T(1,128)}, u32[]{:S(2)}) copy-start(s32[1,32]{1,0:T(1,128)} %param.13) | copy-start | bytes 388
  13.3 73.4 %all-to-all-start = ((bf16[3,8,128,256]{2,3,0,1:T(8,128)(2,1)}), bf16[3,8,128,256]{2,3,0,1:T(8,128)(2,1)S(1)}, u32[]{:S(2)}, u32[]{:S(2)}) async-start(bf16[3,8,128,256]{2,3,0,1:T(8,128)(2,1)} %copy.91), calls=%async_computation | async-start | bytes 3145728 | tf_op jit(solution)/shard_map/all_to_all | solution.py:108
  18.6 118.2 %collective-permute-start.1 = (bf16[256,2048]{1,0:T(8,128)(2,1)}, bf16[256,2048]{1,0:T(8,128)(2,1)}, u32[]{:S(2)}, u32[]{:S(2)}) collective-permute-start(bf16[256,2048]{1,0:T(8,128)(2,1)} %param.11), channel_id=1, source_target_pairs={{0,1},{1,0},{2,3},{3,2},{4,5},{5,4},{6,7},{7,6},{8,9},{9,8},{10,11... | collective-permute-start | bytes 3145736 | tf_op jit(solution)/shard_map/ppermute | solution.py:59
  89.1 2.0 copy-start
  91.0 2.0 copy-start.2
  93.9 3.9 %copy-start.1 = (f32[1024,1024]{0,1:T(8,128)S(1)}, f32[1024,1024]{0,1:T(8,128)}, u32[]{:S(2)}) copy-start(f32[1024,1024]{0,1:T(8,128)} %copy-done) | copy-start | bytes 12582916
  99.9 2.2 copy-start.3
  106.5 3.1 %copy-start.4 = (bf16[1024,128]{0,1:T(8,128)(2,1)S(1)}, bf16[1024,128]{0,1:T(8,128)(2,1)}, u32[]{:S(2)}) copy-start(bf16[1024,128]{0,1:T(8,128)(2,1)} %convolution_convert_fusion.2) | copy-start | bytes 786436
  109.1 24.6 %collective-permute-start = (bf16[1024,256]{0,1:T(8,128)(2,1)S(1)}, bf16[1024,256]{0,1:T(8,128)(2,1)}, u32[]{:S(2)}, u32[]{:S(2)}) collective-permute-start(bf16[1024,256]{0,1:T(8,128)(2,1)S(1)} %get-tuple-element.32), channel_id=1, source_target_pairs={{0,1},{1,0},{2,3},{3,2},{4,5},{5,4},{6,7},{7,6},{8,9},{9,8},{10,11... | collective-permute-start | bytes 1572872 | tf_op jit(solution)/shard_map/ppermute | solution.py:58
  117.0 91.2 %all-to-all-start.1 = ((bf16[8,3,1,128,256]{4,3,1,2,0:T(8,128)(2,1)}), bf16[8,3,1,128,256]{4,3,1,2,0:T(8,128)(2,1)S(1)}, u32[]{:S(2)}, u32[]{:S(2)}) async-start(bf16[8,3,1,128,256]{4,3,1,2,0:T(8,128)(2,1)} %fusion.64), calls=%async_computation.1 | async-start | bytes 3145728 | tf_op jit(solution)/shard_map/all_to_all | solution.py:153
  123.9 63.4 %all-reduce.2.cloned.1.call-start = ((), (), s32[]{:S(2)}) async-start(), calls=%async_computation.2 | async-start | bytes 2097152 | tf_op jit(solution)/shard_map/psum | solution.py:130
  141.8 50.2 %collective-permute-start.2 = (bf16[128,2048]{1,0:T(8,128)(2,1)S(1)}, bf16[128,2048]{1,0:T(8,128)(2,1)}, u32[]{:S(2)}, u32[]{:S(2)}) collective-permute-start(bf16[128,2048]{1,0:T(8,128)(2,1)S(1)} %get-tuple-element.22), channel_id=1, source_target_pairs={{0,2},{1,3},{2,4},{3,5},{4,6},{5,7},{6,0},{7,1},{8,10},{9,11},{10,... | collective-permute-start | bytes 1572872 | tf_op jit(solution)/shard_map/ppermute | solution.py:75
  143.3 59.8 %collective-permute-start.3 = (bf16[128,2048]{1,0:T(8,128)(2,1)S(1)}, bf16[128,2048]{1,0:T(8,128)(2,1)}, u32[]{:S(2)}, u32[]{:S(2)}) collective-permute-start(bf16[128,2048]{1,0:T(8,128)(2,1)S(1)} %get-tuple-element.24), channel_id=1, source_target_pairs={{0,4},{1,5},{2,6},{3,7},{4,0},{5,1},{6,2},{7,3},{8,12},{9,13},{10,... | collective-permute-start | bytes 1572872 | tf_op jit(solution)/shard_map/ppermute | solution.py:75
  144.4 61.0 %collective-permute-start.4 = (bf16[128,2048]{1,0:T(8,128)(2,1)S(1)}, bf16[128,2048]{1,0:T(8,128)(2,1)}, u32[]{:S(2)}, u32[]{:S(2)}) collective-permute-start(bf16[128,2048]{1,0:T(8,128)(2,1)S(1)} %get-tuple-element.23), channel_id=1, source_target_pairs={{0,6},{1,7},{2,0},{3,1},{4,2},{5,3},{6,4},{7,5},{8,14},{9,15},{10,... | collective-permute-start | bytes 1572872 | tf_op jit(solution)/shard_map/ppermute | solution.py:75
Sparse Core Ops, SparseCore 0:
  9.6 77.0 all-gather.2
  133.8 53.4 all-reduce.1
